TPU v7x, 512 devices: a whole 4x4x16 slice. The times are simulated.
512 devices in a mesh: seq: 64 (over z, x_hi, core), section: 8 (over y, x_lo).
Axes of the slice: x: 4 (x_hi: 2, x_lo: 2; x = x_hi * 2 + x_lo), y: 4, z: 16, core: 2. Of those that a mesh axis runs over, the one named last changes fastest.
Arguments:
- fwd_input: bfloat16 [8, 16384, 768], P('section', 'seq'), may hold values from -6 to 6
- bwd_input: bfloat16 [8, 16384, 768], P('section', 'seq'), may hold values from -6 to 6
- bwd_cotangent: bfloat16 [8, 16384, 768], P('section', 'seq'), may hold values from -6 to 6
- conv_weight: bfloat16 [8, 2, 3, 768, 384], P('section', None, None, 'seq'), may hold values from -0.125 to 0.125
- proj_weight: bfloat16 [8, 2, 384, 768], P('section', None, 'seq'), may hold values from -0.3125 to 0.3125
Outputs:
- next_input: bfloat16 [8, 16384, 768], P('section', 'seq')
- prev_cotangent: bfloat16 [8, 16384, 768], P('section', 'seq')
All inputs are finite; a program needn't handle non-finite values.
Results may differ from a plain program's by a relative error of at most 0.012.
Values may be sent and summed in bfloat16 or wider, within the bound.
No kernel may reach another device: no remote copies, remote signals or barrier semaphores. Data moves between devices by JAX's collectives and lax.ppermute only.
A program may use at most 64 MiB of HBM per device.

v0:
```python
import jax
import jax.numpy as jnp
from jax import lax
from jax.sharding import Mesh, PartitionSpec as P

BLOCKS = 2
FIRST_DILATION = 128
SEQ = ("z", "xh", "core")


def seq_size(axis):
    if isinstance(axis, tuple):
        size = 1
        for name in axis:
            size *= lax.axis_size(name)
        return size
    return lax.axis_size(axis)


def padded(x, sides, width):
    for axis, dim in sides:
        size, length = (seq_size(axis), x.shape[dim])
        up = [(i, (i + 1) % size) for i in range(size - 1)]
        down = [(j, i) for i, j in up]
        last = lax.slice_in_dim(x, length - width, length, axis=dim)
        initial = lax.slice_in_dim(x, 0, width, axis=dim)
        before = lax.ppermute(last, axis, up)
        after = lax.ppermute(initial, axis, down)
        x = jnp.concatenate([before, x, after], axis=dim)
    return x


def from_behind(block, axis, distance):
    devices = range(seq_size(axis))
    route = [(i - distance, i) for i in devices if i - distance in devices]
    return lax.ppermute(block, axis, route)


def from_behind_2(block, axis, distance):
    devices = range(seq_size(axis))
    route = [((i - distance) % len(devices), i) for i in devices]
    return lax.ppermute(block, axis, route)


def gelu_back(value, cotangent):
    return jax.vjp(jax.nn.gelu, value)[1](cotangent)[0]


def rounded(product):
    return lax.optimization_barrier(product.astype(jnp.bfloat16)).astype(jnp.float32)


def reach(values, spacing_gap):
    length = values.shape[1]
    if spacing_gap < length:
        padded_input = padded(values, ((SEQ, 1),), spacing_gap)
        return (padded_input[:, :length], padded_input[:, 2 * spacing_gap :])
    shard_hops = spacing_gap // length
    earlier = from_behind(values, SEQ, shard_hops)
    later = from_behind(values, SEQ, -shard_hops)
    return (earlier, later)


def conv_apply(values, weight):
    return jnp.einsum("krc,ch->krh", values, weight, preferred_element_type=jnp.float32)


def conv_transpose(values, weight):
    return jnp.einsum("krh,ch->krc", values, weight, preferred_element_type=jnp.float32)


def run_forward(present_state, pieces):
    stored = []
    for depth_level in range(BLOCKS):
        conv_part, proj_part = pieces[depth_level]
        spacing_gap = FIRST_DILATION * 4**depth_level
        activated = jax.nn.gelu(present_state.astype(jnp.float32)).astype(jnp.bfloat16)
        middle = conv_apply(activated, conv_part[1])
        first_tap = conv_apply(activated, conv_part[0]).astype(jnp.bfloat16)
        last_tap = conv_apply(activated, conv_part[2]).astype(jnp.bfloat16)
        earlier, unused_later = reach(first_tap, spacing_gap)
        unused_earlier, later = reach(last_tap, spacing_gap)
        preact = (
            lax.optimization_barrier(earlier).astype(jnp.float32)
            + middle
            + lax.optimization_barrier(later).astype(jnp.float32)
        )
        hidden = jax.nn.gelu(preact).astype(jnp.bfloat16)
        stored.append((present_state, preact))
        branch = jnp.einsum("krh,hc->krc", hidden, proj_part, preferred_element_type=jnp.float32)
        present_state = (present_state.astype(jnp.float32) + branch).astype(jnp.bfloat16)
    return (present_state, stored)


def place(conv, proj, block, chip, conv_shape, proj_shape):
    rows, split = (block.shape[0], 1)
    for size in conv_shape:
        split *= size
    part = block[:, :split].reshape((rows,) + conv_shape[1:])
    part = jnp.moveaxis(part, 0, 2).reshape(conv_shape[:3] + (rows * conv_shape[3], conv_shape[4]))
    conv = lax.dynamic_update_slice(conv, part, (0, 0, 0, chip * rows * conv_shape[3], 0))
    part = block[:, split:].reshape((rows,) + proj_shape[1:])
    part = jnp.moveaxis(part, 0, 1).reshape(proj_shape[:2] + (rows * proj_shape[2], proj_shape[3]))
    proj = lax.dynamic_update_slice(proj, part, (0, 0, chip * rows * proj_shape[2], 0))
    return (conv, proj)


def gather_weights(conv_weight, proj_weight):
    conv_shape, proj_shape = (conv_weight.shape, proj_weight.shape)
    block = jnp.concatenate([conv_weight.reshape(1, -1), proj_weight.reshape(1, -1)], axis=1)
    block = lax.all_gather(block, "core", axis=0, tiled=True)
    block = lax.all_gather(block, "xh", axis=0, tiled=True)
    span, lanes, cores = (lax.axis_size("z"), lax.axis_size("xh"), lax.axis_size("core"))
    here, core = (lax.axis_index("z"), lax.axis_index("core"))
    sign = 2 * core - 1
    route = []
    for z in range(span):
        for x in range(lanes):
            route.append(((z * lanes + x) * cores, ((z + 1) % span * lanes + x) * cores))
            route.append(((z * lanes + x) * cores + 1, ((z - 1) % span * lanes + x) * cores + 1))
    shards = span * lanes * cores
    conv = jnp.zeros(conv_shape[:3] + (shards * conv_shape[3], conv_shape[4]), conv_weight.dtype)
    proj = jnp.zeros(proj_shape[:2] + (shards * proj_shape[2], proj_shape[3]), proj_weight.dtype)
    conv, proj = place(conv, proj, block, here, conv_shape, proj_shape)
    half = span // 2
    current = block
    for step in range(1, half + 1):
        current = lax.ppermute(current, SEQ, route)
        conv, proj = place(conv, proj, current, (here + sign * step) % span, conv_shape, proj_shape)
        if step < span - half:
            peer = lax.ppermute(current, "core", [(0, 1), (1, 0)])
            conv, proj = place(
                conv, proj, peer, (here - sign * step) % span, conv_shape, proj_shape
            )
    return (conv, proj)


def local(fwd_input, bwd_input, bwd_cotangent, conv_weight, proj_weight):
    convolution_complete, proj_full = gather_weights(conv_weight, proj_weight)
    pieces = [
        (convolution_complete[0, depth_level], proj_full[0, depth_level])
        for depth_level in range(BLOCKS)
    ]
    both_out, both_stored = run_forward(jnp.concatenate([fwd_input, bwd_input], axis=0), pieces)
    forward_out = both_out[:1]
    stored = [(block_in[1:], preact[1:]) for block_in, preact in both_stored]
    cotangent = bwd_cotangent
    for depth_level in reversed(range(BLOCKS)):
        conv_part, proj_part = pieces[depth_level]
        spacing_gap = FIRST_DILATION * 4**depth_level
        block_in, preact = stored[depth_level]
        d_hidden = jnp.einsum(
            "krc,hc->krh", cotangent, proj_part, preferred_element_type=jnp.float32
        )
        d_preact = gelu_back(preact, d_hidden).astype(jnp.bfloat16)
        earlier, later = reach(d_preact, spacing_gap)
        d_act = (
            conv_transpose(later, conv_part[0])
            + conv_transpose(d_preact, conv_part[1])
            + conv_transpose(earlier, conv_part[2])
        )
        total = cotangent.astype(jnp.float32) + gelu_back(block_in.astype(jnp.float32), d_act)
        cotangent = total.astype(jnp.bfloat16)
    next_input = from_behind_2(forward_out, "section", 1)
    prev_cotangent = from_behind_2(cotangent, "section", -1)
    return (next_input, prev_cotangent)


def solution(mesh):
    seq, section = (mesh.shape["seq"], mesh.shape["section"])
    split = Mesh(mesh.devices.reshape(seq // 4, 2, 2, section), SEQ + ("section",))
    in_specs = (
        P("section", SEQ, None),
        P("section", SEQ, None),
        P("section", SEQ, None),
        P("section", None, None, SEQ, None),
        P("section", None, SEQ, None),
    )
    out_specs = (P("section", SEQ, None), P("section", SEQ, None))
    return jax.shard_map(local, mesh=split, in_specs=in_specs, out_specs=out_specs, check_vma=False)
```

profile of v0, /device:TPU:127, one launch (start us, length us, event | category | flops | bytes accessed | tf_op | source)
XLA Modules:
  0.0 322.7 jit_solution(8147360253637598649)
XLA Ops:
  2.4 2.3 all-gather
  5.0 7.2 %all-gather.1 = bf16[2,2,36864]{2,1,0:T(2,128)(2,1)S(1)} all-gather(bf16[1,2,36864]{2,1,0:T(2,128)(2,1)S(1)} %bitcast.209), channel_id=1, replica_groups=mesh['z'=16,'xh'=2,'core'=2,'section'=8] {'xh'}, dimensions={0}, use_global_device_ids=true | all-gather | bytes 442368 | tf_op jit(solution)/shard_map/all_gather | solution.py:112
  13.0 1.9 collective-permute-start
  26.2 1.9 collective-permute-start.2
  28.2 7.2 %collective-permute-start.1 = (bf16[4,36864]{1,0:T(4,128)(2,1)}, bf16[4,36864]{1,0:T(4,128)(2,1)}, u32[]{:S(2)}, u32[]{:S(2)}) collective-permute-start(bf16[4,36864]{1,0:T(4,128)(2,1)} %collective-permute-done), channel_id=1, source_target_pairs={{0,8},{8,0},{1,9},{9,1},{2,10},{10,2},{3,11},{11,3},{4,12},{12,4},... | collective-permute-start | bytes 884744 | tf_op jit(solution)/shard_map/ppermute | solution.py:131
  36.0 1.7 slice.233
  37.7 1.8 reshape.254
  50.1 1.7 slice.234
  51.8 1.8 reshape.256
  56.4 1.9 collective-permute-start.4
  58.3 3.3 %collective-permute-start.3 = (bf16[4,36864]{1,0:T(4,128)(2,1)}, bf16[4,36864]{1,0:T(4,128)(2,1)}, u32[]{:S(2)}, u32[]{:S(2)}) collective-permute-start(bf16[4,36864]{1,0:T(4,128)(2,1)} %collective-permute-done.2), channel_id=1, source_target_pairs={{0,8},{8,0},{1,9},{9,1},{2,10},{10,2},{3,11},{11,3},{4,12},{12,4},... | collective-permute-start | bytes 884744 | tf_op jit(solution)/shard_map/ppermute | solution.py:131
  63.2 1.7 slice.235
  64.9 1.8 reshape.258
  77.3 1.7 slice.236
  79.0 1.8 reshape.260
  83.5 2.4 collective-permute-start.6
  85.9 3.4 %collective-permute-start.5 = (bf16[4,36864]{1,0:T(4,128)(2,1)}, bf16[4,36864]{1,0:T(4,128)(2,1)}, u32[]{:S(2)}, u32[]{:S(2)}) collective-permute-start(bf16[4,36864]{1,0:T(4,128)(2,1)} %collective-permute-done.4), channel_id=1, source_target_pairs={{0,8},{8,0},{1,9},{9,1},{2,10},{10,2},{3,11},{11,3},{4,12},{12,4},... | collective-permute-start | bytes 884744 | tf_op jit(solution)/shard_map/ppermute | solution.py:131
  90.9 1.7 slice.237
  92.6 1.8 reshape.262
  105.0 1.7 slice.238
  106.7 1.8 reshape.264
  111.2 1.9 collective-permute-start.8
  113.1 4.9 %collective-permute-start.7 = (bf16[4,36864]{1,0:T(4,128)(2,1)}, bf16[4,36864]{1,0:T(4,128)(2,1)}, u32[]{:S(2)}, u32[]{:S(2)}) collective-permute-start(bf16[4,36864]{1,0:T(4,128)(2,1)} %collective-permute-done.6), channel_id=1, source_target_pairs={{0,8},{8,0},{1,9},{9,1},{2,10},{10,2},{3,11},{11,3},{4,12},{12,4},... | collective-permute-start | bytes 884744 | tf_op jit(solution)/shard_map/ppermute | solution.py:131
  119.6 1.7 slice.239
  121.3 1.8 reshape.266
  133.7 1.7 slice.240
  135.4 1.8 reshape.268
  139.9 1.9 collective-permute-start.10
  141.8 4.3 %collective-permute-start.9 = (bf16[4,36864]{1,0:T(4,128)(2,1)}, bf16[4,36864]{1,0:T(4,128)(2,1)}, u32[]{:S(2)}, u32[]{:S(2)}) collective-permute-start(bf16[4,36864]{1,0:T(4,128)(2,1)} %collective-permute-done.8), channel_id=1, source_target_pairs={{0,8},{8,0},{1,9},{9,1},{2,10},{10,2},{3,11},{11,3},{4,12},{12,4},... | collective-permute-start | bytes 884744 | tf_op jit(solution)/shard_map/ppermute | solution.py:131
  147.7 1.7 slice.241
  149.4 1.8 reshape.270
  161.8 1.7 slice.242
  163.5 1.8 reshape.272
  168.0 1.9 collective-permute-start.12
  169.9 3.1 collective-permute-start.11
  176.3 1.8 reshape.274
  190.3 1.8 reshape.276
  194.9 2.6 collective-permute-start.14
  197.5 3.7 %collective-permute-start.13 = (bf16[4,36864]{1,0:T(4,128)(2,1)}, bf16[4,36864]{1,0:T(4,128)(2,1)}, u32[]{:S(2)}, u32[]{:S(2)}) collective-permute-start(bf16[4,36864]{1,0:T(4,128)(2,1)} %collective-permute-done.12), channel_id=1, source_target_pairs={{0,8},{8,0},{1,9},{9,1},{2,10},{10,2},{3,11},{11,3},{4,12},{12,4},... | collective-permute-start | bytes 884744 | tf_op jit(solution)/shard_map/ppermute | solution.py:131
  202.7 1.7 slice.245
  204.4 1.8 reshape.278
  207.4 1.7 slice.247
  209.1 1.8 reshape.282
  210.9 1.8 copy.107
  212.7 1.7 slice.246
  214.4 1.8 reshape.280
  218.4 2.6 convolution_convert_fusion.3
  233.9 3.4 %collective-permute-start.15 = (bf16[2,128,384]{2,1,0:T(8,128)(2,1)S(1)}, bf16[2,128,384]{2,1,0:T(8,128)(2,1)S(1)}, u32[]{:S(2)}, u32[]{:S(2)}) collective-permute-start(bf16[2,128,384]{2,1,0:T(8,128)(2,1)S(1)} %slice.249), channel_id=1, source_target_pairs={{0,8},{8,16},{16,24},{24,32},{32,40},{40,48},{48,56},{56,64},{64,7... | collective-permute-start | bytes 589832 | tf_op jit(solution)/shard_map/ppermute | solution.py:27
  238.3 1.9 collective-permute-start.16
  243.4 5.5 %collective-permute-done.16 = bf16[2,128,384]{2,1,0:T(8,128)(2,1)S(1)} collective-permute-done((bf16[2,128,384]{2,1,0:T(8,128)(2,1)S(1)}, bf16[2,128,384]{2,1,0:T(8,128)(2,1)S(1)}, u32[]{:S(2)}, u32[]{:S(2)}) %collective-permute-start.16) | collective-permute-done | bytes 196640 | tf_op jit(solution)/shard_map/ppermute | solution.py:28
  249.1 1.7 fusion.156
  251.5 1.9 collective-permute-start.17
  254.2 4.9 %collective-permute-start.18 = (bf16[2,256,384]{2,1,0:T(8,128)(2,1)S(1)}, bf16[2,256,384]{2,1,0:T(8,128)(2,1)S(1)}, u32[]{:S(2)}, u32[]{:S(2)}) collective-permute-start(bf16[2,256,384]{2,1,0:T(8,128)(2,1)S(1)} %convolution_convert_fusion), channel_id=1, source_target_pairs={{16,0},{24,8},{32,16},{40,24},{48,32},{56,40},{64,48},{72,56},{80,... | collective-permute-start | bytes 1179656 | tf_op jit(solution)/shard_map/ppermute | solution.py:36
  259.8 12.1 %collective-permute-done.17 = bf16[2,256,384]{2,1,0:T(8,128)(2,1)S(1)} collective-permute-done((bf16[2,256,384]{2,1,0:T(8,128)(2,1)S(1)}, bf16[2,256,384]{2,1,0:T(8,128)(2,1)S(1)}, u32[]{:S(2)}, u32[]{:S(2)}) %collective-permute-start.17) | collective-permute-done | bytes 393248 | tf_op jit(solution)/shard_map/ppermute | solution.py:36
  273.6 6.5 %collective-permute-start.21 = (bf16[1,256,384]{2,1,0:T(8,128)(2,1)S(1)}, bf16[1,256,384]{2,1,0:T(8,128)(2,1)S(1)}, u32[]{:S(2)}, u32[]{:S(2)}) collective-permute-start(bf16[1,256,384]{2,1,0:T(8,128)(2,1)S(1)} %fusion.101), channel_id=1, source_target_pairs={{0,16},{8,24},{16,32},{24,40},{32,48},{40,56},{48,64},{56,72},{64,... | collective-permute-start | bytes 589832 | tf_op jit(solution)/shard_map/ppermute | solution.py:36
  280.1 1.9 collective-permute-start.20
  282.0 1.7 fusion.56
  283.9 2.1 collective-permute-start.19
  286.8 4.6 %collective-permute-done.20 = bf16[1,256,384]{2,1,0:T(8,128)(2,1)S(1)} collective-permute-done((bf16[1,256,384]{2,1,0:T(8,128)(2,1)S(1)}, bf16[1,256,384]{2,1,0:T(8,128)(2,1)S(1)}, u32[]{:S(2)}, u32[]{:S(2)}) %collective-permute-start.20) | collective-permute-done | bytes 196640 | tf_op jit(solution)/shard_map/ppermute | solution.py:36
  293.8 5.7 %collective-permute-start.23 = (bf16[1,128,384]{2,1,0:T(8,128)(2,1)S(1)}, bf16[1,128,384]{2,1,0:T(8,128)(2,1)S(1)}, u32[]{:S(2)}, u32[]{:S(2)}) collective-permute-start(bf16[1,128,384]{2,1,0:T(8,128)(2,1)S(1)} %get-tuple-element.3), channel_id=1, source_target_pairs={{0,8},{8,16},{16,24},{24,32},{32,40},{40,48},{48,56},{56,64},{64,7... | collective-permute-start | bytes 294920 | tf_op jit(solution)/shard_map/ppermute | solution.py:27
  299.9 1.9 collective-permute-start.22
  302.2 7.2 %collective-permute-done.22 = bf16[1,128,384]{2,1,0:T(8,128)(2,1)S(1)} collective-permute-done((bf16[1,128,384]{2,1,0:T(8,128)(2,1)S(1)}, bf16[1,128,384]{2,1,0:T(8,128)(2,1)S(1)}, u32[]{:S(2)}, u32[]{:S(2)}) %collective-permute-start.22) | collective-permute-done | bytes 98336 | tf_op jit(solution)/shard_map/ppermute | solution.py:28
  310.2 2.2 collective-permute-start.24
  312.4 8.7 %collective-permute-done.24 = bf16[1,256,768]{2,1,0:T(8,128)(2,1)S(1)} collective-permute-done((bf16[1,256,768]{2,1,0:T(8,128)(2,1)S(1)}, bf16[1,256,768]{2,1,0:T(8,128)(2,1)S(1)}, u32[]{:S(2)}, u32[]{:S(2)}) %collective-permute-start.24) | collective-permute-done | bytes 393248 | tf_op jit(solution)/shard_map/ppermute | solution.py:42
  (167 shorter events, 137.7 us)
Async XLA Ops:
  13.0 9.2 %collective-permute-start = (bf16[4,36864]{1,0:T(4,128)(2,1)}, bf16[4,36864]{1,0:T(4,128)(2,1)}, u32[]{:S(2)}, u32[]{:S(2)}) collective-permute-start(bf16[4,36864]{1,0:T(4,128)(2,1)} %reshape.327), channel_id=1, source_target_pairs={{0,32},{8,488},{16,48},{24,504},{32,64},{40,8},{48,80},{56,24},{64... | collective-permute-start | bytes 884744 | tf_op jit(solution)/shard_map/ppermute | solution.py:128
  19.8 0.9 copy-start.1
  26.2 14.5 %collective-permute-start.2 = (bf16[4,36864]{1,0:T(4,128)(2,1)}, bf16[4,36864]{1,0:T(4,128)(2,1)}, u32[]{:S(2)}, u32[]{:S(2)}) collective-permute-start(bf16[4,36864]{1,0:T(4,128)(2,1)} %collective-permute-done), channel_id=1, source_target_pairs={{0,32},{8,488},{16,48},{24,504},{32,64},{40,8},{48,80},{56,24},{64... | collective-permute-start | bytes 884744 | tf_op jit(solution)/shard_map/ppermute | solution.py:128
  28.2 17.3 %collective-permute-start.1 = (bf16[4,36864]{1,0:T(4,128)(2,1)}, bf16[4,36864]{1,0:T(4,128)(2,1)}, u32[]{:S(2)}, u32[]{:S(2)}) collective-permute-start(bf16[4,36864]{1,0:T(4,128)(2,1)} %collective-permute-done), channel_id=1, source_target_pairs={{0,8},{8,0},{1,9},{9,1},{2,10},{10,2},{3,11},{11,3},{4,12},{12,4},... | collective-permute-start | bytes 884744 | tf_op jit(solution)/shard_map/ppermute | solution.py:131
  56.4 11.5 %collective-permute-start.4 = (bf16[4,36864]{1,0:T(4,128)(2,1)}, bf16[4,36864]{1,0:T(4,128)(2,1)}, u32[]{:S(2)}, u32[]{:S(2)}) collective-permute-start(bf16[4,36864]{1,0:T(4,128)(2,1)} %collective-permute-done.2), channel_id=1, source_target_pairs={{0,32},{8,488},{16,48},{24,504},{32,64},{40,8},{48,80},{56,24},{64... | collective-permute-start | bytes 884744 | tf_op jit(solution)/shard_map/ppermute | solution.py:128
  58.3 14.3 %collective-permute-start.3 = (bf16[4,36864]{1,0:T(4,128)(2,1)}, bf16[4,36864]{1,0:T(4,128)(2,1)}, u32[]{:S(2)}, u32[]{:S(2)}) collective-permute-start(bf16[4,36864]{1,0:T(4,128)(2,1)} %collective-permute-done.2), channel_id=1, source_target_pairs={{0,8},{8,0},{1,9},{9,1},{2,10},{10,2},{3,11},{11,3},{4,12},{12,4},... | collective-permute-start | bytes 884744 | tf_op jit(solution)/shard_map/ppermute | solution.py:131
  83.5 12.1 %collective-permute-start.6 = (bf16[4,36864]{1,0:T(4,128)(2,1)}, bf16[4,36864]{1,0:T(4,128)(2,1)}, u32[]{:S(2)}, u32[]{:S(2)}) collective-permute-start(bf16[4,36864]{1,0:T(4,128)(2,1)} %collective-permute-done.4), channel_id=1, source_target_pairs={{0,32},{8,488},{16,48},{24,504},{32,64},{40,8},{48,80},{56,24},{64... | collective-permute-start | bytes 884744 | tf_op jit(solution)/shard_map/ppermute | solution.py:128
  85.9 14.4 %collective-permute-start.5 = (bf16[4,36864]{1,0:T(4,128)(2,1)}, bf16[4,36864]{1,0:T(4,128)(2,1)}, u32[]{:S(2)}, u32[]{:S(2)}) collective-permute-start(bf16[4,36864]{1,0:T(4,128)(2,1)} %collective-permute-done.4), channel_id=1, source_target_pairs={{0,8},{8,0},{1,9},{9,1},{2,10},{10,2},{3,11},{11,3},{4,12},{12,4},... | collective-permute-start | bytes 884744 | tf_op jit(solution)/shard_map/ppermute | solution.py:131
  111.2 13.1 %collective-permute-start.8 = (bf16[4,36864]{1,0:T(4,128)(2,1)}, bf16[4,36864]{1,0:T(4,128)(2,1)}, u32[]{:S(2)}, u32[]{:S(2)}) collective-permute-start(bf16[4,36864]{1,0:T(4,128)(2,1)} %collective-permute-done.6), channel_id=1, source_target_pairs={{0,32},{8,488},{16,48},{24,504},{32,64},{40,8},{48,80},{56,24},{64... | collective-permute-start | bytes 884744 | tf_op jit(solution)/shard_map/ppermute | solution.py:128
  113.1 15.8 %collective-permute-start.7 = (bf16[4,36864]{1,0:T(4,128)(2,1)}, bf16[4,36864]{1,0:T(4,128)(2,1)}, u32[]{:S(2)}, u32[]{:S(2)}) collective-permute-start(bf16[4,36864]{1,0:T(4,128)(2,1)} %collective-permute-done.6), channel_id=1, source_target_pairs={{0,8},{8,0},{1,9},{9,1},{2,10},{10,2},{3,11},{11,3},{4,12},{12,4},... | collective-permute-start | bytes 884744 | tf_op jit(solution)/shard_map/ppermute | solution.py:131
  139.9 12.5 %collective-permute-start.10 = (bf16[4,36864]{1,0:T(4,128)(2,1)}, bf16[4,36864]{1,0:T(4,128)(2,1)}, u32[]{:S(2)}, u32[]{:S(2)}) collective-permute-start(bf16[4,36864]{1,0:T(4,128)(2,1)} %collective-permute-done.8), channel_id=1, source_target_pairs={{0,32},{8,488},{16,48},{24,504},{32,64},{40,8},{48,80},{56,24},{64... | collective-permute-start | bytes 884744 | tf_op jit(solution)/shard_map/ppermute | solution.py:128
  141.8 15.3 %collective-permute-start.9 = (bf16[4,36864]{1,0:T(4,128)(2,1)}, bf16[4,36864]{1,0:T(4,128)(2,1)}, u32[]{:S(2)}, u32[]{:S(2)}) collective-permute-start(bf16[4,36864]{1,0:T(4,128)(2,1)} %collective-permute-done.8), channel_id=1, source_target_pairs={{0,8},{8,0},{1,9},{9,1},{2,10},{10,2},{3,11},{11,3},{4,12},{12,4},... | collective-permute-start | bytes 884744 | tf_op jit(solution)/shard_map/ppermute | solution.py:131
  168.0 11.3 %collective-permute-start.12 = (bf16[4,36864]{1,0:T(4,128)(2,1)}, bf16[4,36864]{1,0:T(4,128)(2,1)}, u32[]{:S(2)}, u32[]{:S(2)}) collective-permute-start(bf16[4,36864]{1,0:T(4,128)(2,1)} %collective-permute-done.10), channel_id=1, source_target_pairs={{0,32},{8,488},{16,48},{24,504},{32,64},{40,8},{48,80},{56,24},{64... | collective-permute-start | bytes 884744 | tf_op jit(solution)/shard_map/ppermute | solution.py:128
  169.9 14.0 %collective-permute-start.11 = (bf16[4,36864]{1,0:T(4,128)(2,1)}, bf16[4,36864]{1,0:T(4,128)(2,1)}, u32[]{:S(2)}, u32[]{:S(2)}) collective-permute-start(bf16[4,36864]{1,0:T(4,128)(2,1)} %collective-permute-done.10), channel_id=1, source_target_pairs={{0,8},{8,0},{1,9},{9,1},{2,10},{10,2},{3,11},{11,3},{4,12},{12,4},... | collective-permute-start | bytes 884744 | tf_op jit(solution)/shard_map/ppermute | solution.py:131
  194.9 12.5 %collective-permute-start.14 = (bf16[4,36864]{1,0:T(4,128)(2,1)}, bf16[4,36864]{1,0:T(4,128)(2,1)}, u32[]{:S(2)}, u32[]{:S(2)}) collective-permute-start(bf16[4,36864]{1,0:T(4,128)(2,1)} %collective-permute-done.12), channel_id=1, source_target_pairs={{0,32},{8,488},{16,48},{24,504},{32,64},{40,8},{48,80},{56,24},{64... | collective-permute-start | bytes 884744 | tf_op jit(solution)/shard_map/ppermute | solution.py:128
  197.5 15.2 %collective-permute-start.13 = (bf16[4,36864]{1,0:T(4,128)(2,1)}, bf16[4,36864]{1,0:T(4,128)(2,1)}, u32[]{:S(2)}, u32[]{:S(2)}) collective-permute-start(bf16[4,36864]{1,0:T(4,128)(2,1)} %collective-permute-done.12), channel_id=1, source_target_pairs={{0,8},{8,0},{1,9},{9,1},{2,10},{10,2},{3,11},{11,3},{4,12},{12,4},... | collective-permute-start | bytes 884744 | tf_op jit(solution)/shard_map/ppermute | solution.py:131
  218.4 2.7 copy-start.3
  218.4 2.7 copy-start.6
  231.9 16.9 %copy-start = (bf16[2,256,384]{2,1,0:T(8,128)(2,1)S(1)}, bf16[2,256,384]{2,1,0:T(8,128)(2,1)}, u32[]{:S(2)}) copy-start(bf16[2,256,384]{2,1,0:T(8,128)(2,1)} %convolution_convert_fusion.2) | copy-start | bytes 1179652
  231.9 17.0 %copy-start.2 = (f32[2,256,384]{2,1,0:T(8,128)S(1)}, f32[2,256,384]{2,1,0:T(8,128)}, u32[]{:S(2)}) copy-start(f32[2,256,384]{2,1,0:T(8,128)} %fusion.64) | copy-start | bytes 2359300
  233.9 8.4 %collective-permute-start.15 = (bf16[2,128,384]{2,1,0:T(8,128)(2,1)S(1)}, bf16[2,128,384]{2,1,0:T(8,128)(2,1)S(1)}, u32[]{:S(2)}, u32[]{:S(2)}) collective-permute-start(bf16[2,128,384]{2,1,0:T(8,128)(2,1)S(1)} %slice.249), channel_id=1, source_target_pairs={{0,8},{8,16},{16,24},{24,32},{32,40},{40,48},{48,56},{56,64},{64,7... | collective-permute-start | bytes 589832 | tf_op jit(solution)/shard_map/ppermute | solution.py:27
  238.3 10.6 %collective-permute-start.16 = (bf16[2,128,384]{2,1,0:T(8,128)(2,1)S(1)}, bf16[2,128,384]{2,1,0:T(8,128)(2,1)S(1)}, u32[]{:S(2)}, u32[]{:S(2)}) collective-permute-start(bf16[2,128,384]{2,1,0:T(8,128)(2,1)S(1)} %slice.252), channel_id=1, source_target_pairs={{8,0},{16,8},{24,16},{32,24},{40,32},{48,40},{56,48},{64,56},{72,6... | collective-permute-start | bytes 589832 | tf_op jit(solution)/shard_map/ppermute | solution.py:28
  243.3 5.7 %copy-start.4 = (bf16[1,256,768]{2,1,0:T(8,128)(2,1)S(1)}, bf16[1,256,768]{2,1,0:T(8,128)(2,1)}, u32[]{:S(2)}) copy-start(bf16[1,256,768]{2,1,0:T(8,128)(2,1)} %param.5) | copy-start | bytes 1179652
  243.4 5.7 %copy-start.7 = (bf16[1,256,768]{2,1,0:T(8,128)(2,1)S(1)}, bf16[1,256,768]{2,1,0:T(8,128)(2,1)}, u32[]{:S(2)}) copy-start(bf16[1,256,768]{2,1,0:T(8,128)(2,1)} %param.6) | copy-start | bytes 1179652
  251.5 20.3 %collective-permute-start.17 = (bf16[2,256,384]{2,1,0:T(8,128)(2,1)S(1)}, bf16[2,256,384]{2,1,0:T(8,128)(2,1)S(1)}, u32[]{:S(2)}, u32[]{:S(2)}) collective-permute-start(bf16[2,256,384]{2,1,0:T(8,128)(2,1)S(1)} %convolution_convert_fusion.1), channel_id=1, source_target_pairs={{0,16},{8,24},{16,32},{24,40},{32,48},{40,56},{48,64},{56,72},{64,... | collective-permute-start | bytes 1179656 | tf_op jit(solution)/shard_map/ppermute | solution.py:36
  254.2 17.7 %collective-permute-start.18 = (bf16[2,256,384]{2,1,0:T(8,128)(2,1)S(1)}, bf16[2,256,384]{2,1,0:T(8,128)(2,1)S(1)}, u32[]{:S(2)}, u32[]{:S(2)}) collective-permute-start(bf16[2,256,384]{2,1,0:T(8,128)(2,1)S(1)} %convolution_convert_fusion), channel_id=1, source_target_pairs={{16,0},{24,8},{32,16},{40,24},{48,32},{56,40},{64,48},{72,56},{80,... | collective-permute-start | bytes 1179656 | tf_op jit(solution)/shard_map/ppermute | solution.py:36
  259.8 12.2 %copy-start.5 = (bf16[1,256,768]{2,1,0:T(8,128)(2,1)S(1)}, bf16[1,256,768]{2,1,0:T(8,128)(2,1)}, u32[]{:S(2)}) copy-start(bf16[1,256,768]{2,1,0:T(8,128)(2,1)} %param.7) | copy-start | bytes 1179652
  273.6 12.8 %collective-permute-start.21 = (bf16[1,256,384]{2,1,0:T(8,128)(2,1)S(1)}, bf16[1,256,384]{2,1,0:T(8,128)(2,1)S(1)}, u32[]{:S(2)}, u32[]{:S(2)}) collective-permute-start(bf16[1,256,384]{2,1,0:T(8,128)(2,1)S(1)} %fusion.101), channel_id=1, source_target_pairs={{0,16},{8,24},{16,32},{24,40},{32,48},{40,56},{48,64},{56,72},{64,... | collective-permute-start | bytes 589832 | tf_op jit(solution)/shard_map/ppermute | solution.py:36
  280.1 11.3 %collective-permute-start.20 = (bf16[1,256,384]{2,1,0:T(8,128)(2,1)S(1)}, bf16[1,256,384]{2,1,0:T(8,128)(2,1)S(1)}, u32[]{:S(2)}, u32[]{:S(2)}) collective-permute-start(bf16[1,256,384]{2,1,0:T(8,128)(2,1)S(1)} %fusion.101), channel_id=1, source_target_pairs={{16,0},{24,8},{32,16},{40,24},{48,32},{56,40},{64,48},{72,56},{80,... | collective-permute-start | bytes 589832 | tf_op jit(solution)/shard_map/ppermute | solution.py:36
  283.9 28.6 %collective-permute-start.19 = (bf16[1,256,768]{2,1,0:T(8,128)(2,1)S(1)}, bf16[1,256,768]{2,1,0:T(8,128)(2,1)S(1)}, u32[]{:S(2)}, u32[]{:S(2)}) collective-permute-start(bf16[1,256,768]{2,1,0:T(8,128)(2,1)S(1)} %fusion.55), channel_id=1, source_target_pairs={{7,0},{0,1},{1,2},{2,3},{3,4},{4,5},{5,6},{6,7},{15,8},{8,9},{9,10... | collective-permute-start | bytes 1179656 | tf_op jit(solution)/shard_map/ppermute | solution.py:42
  293.8 8.0 %collective-permute-start.23 = (bf16[1,128,384]{2,1,0:T(8,128)(2,1)S(1)}, bf16[1,128,384]{2,1,0:T(8,128)(2,1)S(1)}, u32[]{:S(2)}, u32[]{:S(2)}) collective-permute-start(bf16[1,128,384]{2,1,0:T(8,128)(2,1)S(1)} %get-tuple-element.3), channel_id=1, source_target_pairs={{0,8},{8,16},{16,24},{24,32},{32,40},{40,48},{48,56},{56,64},{64,7... | collective-permute-start | bytes 294920 | tf_op jit(solution)/shard_map/ppermute | solution.py:27
  299.9 9.5 %collective-permute-start.22 = (bf16[1,128,384]{2,1,0:T(8,128)(2,1)S(1)}, bf16[1,128,384]{2,1,0:T(8,128)(2,1)S(1)}, u32[]{:S(2)}, u32[]{:S(2)}) collective-permute-start(bf16[1,128,384]{2,1,0:T(8,128)(2,1)S(1)} %get-tuple-element.2), channel_id=1, source_target_pairs={{8,0},{16,8},{24,16},{32,24},{40,32},{48,40},{56,48},{64,56},{72,6... | collective-permute-start | bytes 294920 | tf_op jit(solution)/shard_map/ppermute | solution.py:28
  310.2 10.9 %collective-permute-start.24 = (bf16[1,256,768]{2,1,0:T(8,128)(2,1)S(1)}, bf16[1,256,768]{2,1,0:T(8,128)(2,1)S(1)}, u32[]{:S(2)}, u32[]{:S(2)}) collective-permute-start(bf16[1,256,768]{2,1,0:T(8,128)(2,1)S(1)} %fusion.24), channel_id=1, source_target_pairs={{1,0},{2,1},{3,2},{4,3},{5,4},{6,5},{7,6},{0,7},{9,8},{10,9},{11,1... | collective-permute-start | bytes 1179656 | tf_op jit(solution)/shard_map/ppermute | solution.py:42
where the time goes:
time: 328 us; the launch traced here: 323 us
  local copies, waits for them, and re-layouts  174 us (53%)
  starting transfers between devices  79 us (24%)
  waiting for transfers between devices  39.6 us (12%)
  matrix products  17.6 us (5%)
  blocking collectives  9.53 us (3%)
    ppermute x7, starting transfers between devices, gather_weights(): peer = lax.ppermute(current, 'core', [(0, 1), (1, 0)])  30 us
    reshape x16, local copies, waits for them, and re-layouts, place(): part = block[:, :split].reshape((rows,) + conv_shape[1:])  27.1 us
    slice x16, local copies, waits for them, and re-layouts, place(): part = block[:, :split].reshape((rows,) + conv_shape[1:])  26.5 us
    slice x16, local copies, waits for them, and re-layouts, place(): part = block[:, split:].reshape((rows,) + proj_shape[1:])  24.1 us
    reshape x16, local copies, waits for them, and re-layouts, place(): part = block[:, split:].reshape((rows,) + proj_shape[1:])  23.7 us
    transpose x16, local copies, waits for them, and re-layouts, place(): jnp.moveaxis(part, 0, 1)  22.5 us
    dynamic_update_slice x16, local copies, waits for them, and re-layouts, place(): lax.dynamic_update_slice(proj, part, (0, 0, chip * rows * proj_shape[2], 0))  21.8 us
    transpose x16, local copies, waits for them, and re-layouts, place(): jnp.moveaxis(part, 0, 2)  18.5 us
  transfers between devices with their start and end apart: 25, of which 6 were waited for; matrix products, arithmetic and copies ran while one was open for 29% of the time, Pallas kernels for 0%

commit v1 on v0

--- a/solution.py
+++ b/solution.py
@@ -6,6 +6,19 @@
 BLOCKS = 2
 FIRST_DILATION = 128
 SEQ = ("z", "xh", "core")
+
+
+def prepare_wires(x_part, on_dim):
+    state_next = jnp.concatenate(
+        lax.all_to_all(
+            jnp.stack(lax.psum(1, axis_name="xh") * [x_part]),
+            axis_name="xh",
+            split_axis=0,
+            concat_axis=0,
+        ),
+        on_dim,
+    )
+    return state_next
 
 
 def seq_size(axis):
@@ -109,7 +122,7 @@
     conv_shape, proj_shape = (conv_weight.shape, proj_weight.shape)
     block = jnp.concatenate([conv_weight.reshape(1, -1), proj_weight.reshape(1, -1)], axis=1)
     block = lax.all_gather(block, "core", axis=0, tiled=True)
-    block = lax.all_gather(block, "xh", axis=0, tiled=True)
+    block = prepare_wires(block, 0)
     span, lanes, cores = (lax.axis_size("z"), lax.axis_size("xh"), lax.axis_size("core"))
     here, core = (lax.axis_index("z"), lax.axis_index("core"))
     sign = 2 * core - 1

time: 328 us -> 333 us (1.015)
  starting transfers between devices: 79 us -> 86.9 us
  blocking collectives: 9.53 us -> 2.33 us
  waiting for transfers between devices: 39.6 us -> 44.2 us
    all_gather x1 -> x0, blocking collectives: 7.2 us -> none  [gather_weights(): block = lax.all_gather(block, 'xh', axis=0, tiled=True)]
    all_to_all x0 -> x1, starting transfers between devices: none -> 4.56 us  [prepare_wires(): lax.all_to_all(jnp.stack(lax.psum(1, axis_name='xh') * [x_part]), axis_na...]
    all_to_all x0 -> x1, waiting for transfers between devices: none -> 4.08 us  [prepare_wires(): lax.all_to_all(jnp.stack(lax.psum(1, axis_name='xh') * [x_part]), axis_na...]
  transfers between devices with their start and end apart: 25 -> 26, of which waited for: 6 -> 8; matrix products, arithmetic and copies ran while one was open for 29% -> 28% of each run, Pallas kernels for 0% -> 0%
where the time goes in v1:
time: 333 us; the launch traced here: 328 us
  local copies, waits for them, and re-layouts  173 us (52%)
  starting transfers between devices  86.9 us (26%)
  waiting for transfers between devices  44.2 us (13%)
  matrix products  17.6 us (5%)
    ppermute x7, starting transfers between devices, gather_weights(): peer = lax.ppermute(current, 'core', [(0, 1), (1, 0)])  29 us
    reshape x16, local copies, waits for them, and re-layouts, place(): part = block[:, :split].reshape((rows,) + conv_shape[1:])  27.1 us
    slice x16, local copies, waits for them, and re-layouts, place(): part = block[:, :split].reshape((rows,) + conv_shape[1:])  26.5 us
    slice x16, local copies, waits for them, and re-layouts, place(): part = block[:, split:].reshape((rows,) + proj_shape[1:])  24 us
    reshape x16, local copies, waits for them, and re-layouts, place(): part = block[:, split:].reshape((rows,) + proj_shape[1:])  23.7 us
    transpose x16, local copies, waits for them, and re-layouts, place(): jnp.moveaxis(part, 0, 1)  22.6 us
    dynamic_update_slice x16, local copies, waits for them, and re-layouts, place(): lax.dynamic_update_slice(proj, part, (0, 0, chip * rows * proj_shape[2], 0))  21.8 us
    transpose x16, local copies, waits for them, and re-layouts, place(): jnp.moveaxis(part, 0, 2)  17.9 us
  transfers between devices with their start and end apart: 26, of which 8 were waited for; matrix products, arithmetic and copies ran while one was open for 28% of the time, Pallas kernels for 0%

profile of v1, /device:TPU:127, one launch (start us, length us, event | category | flops | bytes accessed | tf_op | source)
XLA Modules:
  0.0 327.6 jit_solution(8818311237300937818)
XLA Ops:
  2.4 2.3 all-gather
  6.0 4.6 %all-to-all-start = ((bf16[2,2,36864]{2,1,0:T(2,128)(2,1)}), bf16[2,2,36864]{2,1,0:T(2,128)(2,1)S(1)}, u32[]{:S(2)}, u32[]{:S(2)}) async-start(bf16[2,2,36864]{2,1,0:T(2,128)(2,1)} %pad_maximum_fusion.3), calls=%async_computation | async-start | bytes 589824 | tf_op jit(solution)/shard_map/all_to_all | solution.py:13
  10.5 4.1 %all-to-all-done = bf16[2,2,36864]{2,1,0:T(2,128)(2,1)S(1)} async-done(((bf16[2,2,36864]{2,1,0:T(2,128)(2,1)}), bf16[2,2,36864]{2,1,0:T(2,128)(2,1)S(1)}, u32[]{:S(2)}, u32[]{:S(2)}) %all-to-all-start) | async-done | bytes 294944 | tf_op jit(solution)/shard_map/all_to_all | solution.py:13
  16.3 1.9 collective-permute-start
  21.9 3.6 %collective-permute-done = bf16[4,36864]{1,0:T(4,128)(2,1)} collective-permute-done((bf16[4,36864]{1,0:T(4,128)(2,1)}, bf16[4,36864]{1,0:T(4,128)(2,1)}, u32[]{:S(2)}, u32[]{:S(2)}) %collective-permute-start) | collective-permute-done | bytes 294944 | tf_op jit(solution)/shard_map/ppermute | solution.py:141
  29.6 1.9 collective-permute-start.2
  31.5 6.9 %collective-permute-start.1 = (bf16[4,36864]{1,0:T(4,128)(2,1)}, bf16[4,36864]{1,0:T(4,128)(2,1)}, u32[]{:S(2)}, u32[]{:S(2)}) collective-permute-start(bf16[4,36864]{1,0:T(4,128)(2,1)} %collective-permute-done), channel_id=1, source_target_pairs={{0,8},{8,0},{1,9},{9,1},{2,10},{10,2},{3,11},{11,3},{4,12},{12,4},... | collective-permute-start | bytes 884744 | tf_op jit(solution)/shard_map/ppermute | solution.py:144
  39.1 1.7 slice.233
  40.8 1.8 reshape.258
  53.2 1.7 slice.234
  54.9 1.8 reshape.260
  59.4 1.9 collective-permute-start.4
  61.3 2.9 collective-permute-start.3
  65.8 1.7 slice.235
  67.5 1.8 reshape.262
  79.9 1.7 slice.236
  81.5 1.8 reshape.264
  86.1 2.7 collective-permute-start.6
  88.7 3.6 %collective-permute-start.5 = (bf16[4,36864]{1,0:T(4,128)(2,1)}, bf16[4,36864]{1,0:T(4,128)(2,1)}, u32[]{:S(2)}, u32[]{:S(2)}) collective-permute-start(bf16[4,36864]{1,0:T(4,128)(2,1)} %collective-permute-done.4), channel_id=1, source_target_pairs={{0,8},{8,0},{1,9},{9,1},{2,10},{10,2},{3,11},{11,3},{4,12},{12,4},... | collective-permute-start | bytes 884744 | tf_op jit(solution)/shard_map/ppermute | solution.py:144
  93.9 1.7 slice.237
  95.6 1.8 reshape.266
  108.0 1.7 slice.238
  109.7 1.8 reshape.268
  114.2 2.0 collective-permute-start.8
  116.2 3.6 %collective-permute-start.7 = (bf16[4,36864]{1,0:T(4,128)(2,1)}, bf16[4,36864]{1,0:T(4,128)(2,1)}, u32[]{:S(2)}, u32[]{:S(2)}) collective-permute-start(bf16[4,36864]{1,0:T(4,128)(2,1)} %collective-permute-done.6), channel_id=1, source_target_pairs={{0,8},{8,0},{1,9},{9,1},{2,10},{10,2},{3,11},{11,3},{4,12},{12,4},... | collective-permute-start | bytes 884744 | tf_op jit(solution)/shard_map/ppermute | solution.py:144
  121.3 1.7 slice.239
  123.0 1.8 reshape.270
  135.4 1.7 slice.240
  137.1 1.8 reshape.272
  141.6 2.3 collective-permute-start.10
  144.0 5.2 %collective-permute-start.9 = (bf16[4,36864]{1,0:T(4,128)(2,1)}, bf16[4,36864]{1,0:T(4,128)(2,1)}, u32[]{:S(2)}, u32[]{:S(2)}) collective-permute-start(bf16[4,36864]{1,0:T(4,128)(2,1)} %collective-permute-done.8), channel_id=1, source_target_pairs={{0,8},{8,0},{1,9},{9,1},{2,10},{10,2},{3,11},{11,3},{4,12},{12,4},... | collective-permute-start | bytes 884744 | tf_op jit(solution)/shard_map/ppermute | solution.py:144
  152.4 1.8 reshape.274
  166.5 1.8 reshape.276
  171.0 1.9 collective-permute-start.12
  172.9 3.1 collective-permute-start.11
  179.3 1.8 reshape.278
  193.4 1.8 reshape.280
  197.9 2.6 collective-permute-start.14
  200.5 3.6 %collective-permute-start.13 = (bf16[4,36864]{1,0:T(4,128)(2,1)}, bf16[4,36864]{1,0:T(4,128)(2,1)}, u32[]{:S(2)}, u32[]{:S(2)}) collective-permute-start(bf16[4,36864]{1,0:T(4,128)(2,1)} %collective-permute-done.12), channel_id=1, source_target_pairs={{0,8},{8,0},{1,9},{9,1},{2,10},{10,2},{3,11},{11,3},{4,12},{12,4},... | collective-permute-start | bytes 884744 | tf_op jit(solution)/shard_map/ppermute | solution.py:144
  207.4 1.8 reshape.282
  210.4 1.7 slice.247
  212.1 1.8 reshape.286
  213.9 1.8 copy.107
  215.7 1.7 slice.246
  217.4 1.8 reshape.284
  221.4 2.6 convolution_convert_fusion.3
  236.9 5.3 %collective-permute-start.15 = (bf16[2,128,384]{2,1,0:T(8,128)(2,1)S(1)}, bf16[2,128,384]{2,1,0:T(8,128)(2,1)S(1)}, u32[]{:S(2)}, u32[]{:S(2)}) collective-permute-start(bf16[2,128,384]{2,1,0:T(8,128)(2,1)S(1)} %slice.249), channel_id=1, source_target_pairs={{0,8},{8,16},{16,24},{24,32},{32,40},{40,48},{48,56},{56,64},{64,7... | collective-permute-start | bytes 589832 | tf_op jit(solution)/shard_map/ppermute | solution.py:40
  243.1 1.9 collective-permute-start.16
  248.2 5.5 %collective-permute-done.16 = bf16[2,128,384]{2,1,0:T(8,128)(2,1)S(1)} collective-permute-done((bf16[2,128,384]{2,1,0:T(8,128)(2,1)S(1)}, bf16[2,128,384]{2,1,0:T(8,128)(2,1)S(1)}, u32[]{:S(2)}, u32[]{:S(2)}) %collective-permute-start.16) | collective-permute-done | bytes 196640 | tf_op jit(solution)/shard_map/ppermute | solution.py:41
  253.9 1.7 fusion.156
  256.4 1.9 collective-permute-start.17
  259.0 4.9 %collective-permute-start.18 = (bf16[2,256,384]{2,1,0:T(8,128)(2,1)S(1)}, bf16[2,256,384]{2,1,0:T(8,128)(2,1)S(1)}, u32[]{:S(2)}, u32[]{:S(2)}) collective-permute-start(bf16[2,256,384]{2,1,0:T(8,128)(2,1)S(1)} %convolution_convert_fusion), channel_id=1, source_target_pairs={{16,0},{24,8},{32,16},{40,24},{48,32},{56,40},{64,48},{72,56},{80,... | collective-permute-start | bytes 1179656 | tf_op jit(solution)/shard_map/ppermute | solution.py:49
  264.6 2.4 collective-permute-done.17
  267.0 7.9 %collective-permute-done.18 = bf16[2,256,384]{2,1,0:T(8,128)(2,1)S(1)} collective-permute-done((bf16[2,256,384]{2,1,0:T(8,128)(2,1)S(1)}, bf16[2,256,384]{2,1,0:T(8,128)(2,1)S(1)}, u32[]{:S(2)}, u32[]{:S(2)}) %collective-permute-start.18) | collective-permute-done | bytes 393248 | tf_op jit(solution)/shard_map/ppermute | solution.py:49
  276.6 8.3 %collective-permute-start.21 = (bf16[1,256,384]{2,1,0:T(8,128)(2,1)S(1)}, bf16[1,256,384]{2,1,0:T(8,128)(2,1)S(1)}, u32[]{:S(2)}, u32[]{:S(2)}) collective-permute-start(bf16[1,256,384]{2,1,0:T(8,128)(2,1)S(1)} %fusion.101), channel_id=1, source_target_pairs={{0,16},{8,24},{16,32},{24,40},{32,48},{40,56},{48,64},{56,72},{64,... | collective-permute-start | bytes 589832 | tf_op jit(solution)/shard_map/ppermute | solution.py:49
  285.0 1.9 collective-permute-start.20
  286.9 1.7 fusion.56
  288.7 2.1 collective-permute-start.19
  291.7 4.6 %collective-permute-done.20 = bf16[1,256,384]{2,1,0:T(8,128)(2,1)S(1)} collective-permute-done((bf16[1,256,384]{2,1,0:T(8,128)(2,1)S(1)}, bf16[1,256,384]{2,1,0:T(8,128)(2,1)S(1)}, u32[]{:S(2)}, u32[]{:S(2)}) %collective-permute-start.20) | collective-permute-done | bytes 196640 | tf_op jit(solution)/shard_map/ppermute | solution.py:49
  298.7 5.7 %collective-permute-start.23 = (bf16[1,128,384]{2,1,0:T(8,128)(2,1)S(1)}, bf16[1,128,384]{2,1,0:T(8,128)(2,1)S(1)}, u32[]{:S(2)}, u32[]{:S(2)}) collective-permute-start(bf16[1,128,384]{2,1,0:T(8,128)(2,1)S(1)} %get-tuple-element.3), channel_id=1, source_target_pairs={{0,8},{8,16},{16,24},{24,32},{32,40},{40,48},{48,56},{56,64},{64,7... | collective-permute-start | bytes 294920 | tf_op jit(solution)/shard_map/ppermute | solution.py:40
  304.8 1.9 collective-permute-start.22
  307.1 7.3 %collective-permute-done.22 = bf16[1,128,384]{2,1,0:T(8,128)(2,1)S(1)} collective-permute-done((bf16[1,128,384]{2,1,0:T(8,128)(2,1)S(1)}, bf16[1,128,384]{2,1,0:T(8,128)(2,1)S(1)}, u32[]{:S(2)}, u32[]{:S(2)}) %collective-permute-start.22) | collective-permute-done | bytes 98336 | tf_op jit(solution)/shard_map/ppermute | solution.py:41
  315.2 2.1 collective-permute-start.24
  317.3 8.7 %collective-permute-done.24 = bf16[1,256,768]{2,1,0:T(8,128)(2,1)S(1)} collective-permute-done((bf16[1,256,768]{2,1,0:T(8,128)(2,1)S(1)}, bf16[1,256,768]{2,1,0:T(8,128)(2,1)S(1)}, u32[]{:S(2)}, u32[]{:S(2)}) %collective-permute-start.24) | collective-permute-done | bytes 393248 | tf_op jit(solution)/shard_map/ppermute | solution.py:55
  (167 shorter events, 140.9 us)
Async XLA Ops:
  6.0 8.6 %all-to-all-start = ((bf16[2,2,36864]{2,1,0:T(2,128)(2,1)}), bf16[2,2,36864]{2,1,0:T(2,128)(2,1)S(1)}, u32[]{:S(2)}, u32[]{:S(2)}) async-start(bf16[2,2,36864]{2,1,0:T(2,128)(2,1)} %pad_maximum_fusion.3), calls=%async_computation | async-start | bytes 589824 | tf_op jit(solution)/shard_map/all_to_all | solution.py:13
  16.3 9.2 %collective-permute-start = (bf16[4,36864]{1,0:T(4,128)(2,1)}, bf16[4,36864]{1,0:T(4,128)(2,1)}, u32[]{:S(2)}, u32[]{:S(2)}) collective-permute-start(bf16[4,36864]{1,0:T(4,128)(2,1)} %reshape.255), channel_id=1, source_target_pairs={{0,32},{8,488},{16,48},{24,504},{32,64},{40,8},{48,80},{56,24},{64... | collective-permute-start | bytes 884744 | tf_op jit(solution)/shard_map/ppermute | solution.py:141
  29.6 14.2 %collective-permute-start.2 = (bf16[4,36864]{1,0:T(4,128)(2,1)}, bf16[4,36864]{1,0:T(4,128)(2,1)}, u32[]{:S(2)}, u32[]{:S(2)}) collective-permute-start(bf16[4,36864]{1,0:T(4,128)(2,1)} %collective-permute-done), channel_id=1, source_target_pairs={{0,32},{8,488},{16,48},{24,504},{32,64},{40,8},{48,80},{56,24},{64... | collective-permute-start | bytes 884744 | tf_op jit(solution)/shard_map/ppermute | solution.py:141
  31.5 17.0 %collective-permute-start.1 = (bf16[4,36864]{1,0:T(4,128)(2,1)}, bf16[4,36864]{1,0:T(4,128)(2,1)}, u32[]{:S(2)}, u32[]{:S(2)}) collective-permute-start(bf16[4,36864]{1,0:T(4,128)(2,1)} %collective-permute-done), channel_id=1, source_target_pairs={{0,8},{8,0},{1,9},{9,1},{2,10},{10,2},{3,11},{11,3},{4,12},{12,4},... | collective-permute-start | bytes 884744 | tf_op jit(solution)/shard_map/ppermute | solution.py:144
  59.4 11.0 %collective-permute-start.4 = (bf16[4,36864]{1,0:T(4,128)(2,1)}, bf16[4,36864]{1,0:T(4,128)(2,1)}, u32[]{:S(2)}, u32[]{:S(2)}) collective-permute-start(bf16[4,36864]{1,0:T(4,128)(2,1)} %collective-permute-done.2), channel_id=1, source_target_pairs={{0,32},{8,488},{16,48},{24,504},{32,64},{40,8},{48,80},{56,24},{64... | collective-permute-start | bytes 884744 | tf_op jit(solution)/shard_map/ppermute | solution.py:141
  61.3 13.8 %collective-permute-start.3 = (bf16[4,36864]{1,0:T(4,128)(2,1)}, bf16[4,36864]{1,0:T(4,128)(2,1)}, u32[]{:S(2)}, u32[]{:S(2)}) collective-permute-start(bf16[4,36864]{1,0:T(4,128)(2,1)} %collective-permute-done.2), channel_id=1, source_target_pairs={{0,8},{8,0},{1,9},{9,1},{2,10},{10,2},{3,11},{11,3},{4,12},{12,4},... | collective-permute-start | bytes 884744 | tf_op jit(solution)/shard_map/ppermute | solution.py:144
  86.1 12.5 %collective-permute-start.6 = (bf16[4,36864]{1,0:T(4,128)(2,1)}, bf16[4,36864]{1,0:T(4,128)(2,1)}, u32[]{:S(2)}, u32[]{:S(2)}) collective-permute-start(bf16[4,36864]{1,0:T(4,128)(2,1)} %collective-permute-done.4), channel_id=1, source_target_pairs={{0,32},{8,488},{16,48},{24,504},{32,64},{40,8},{48,80},{56,24},{64... | collective-permute-start | bytes 884744 | tf_op jit(solution)/shard_map/ppermute | solution.py:141
  88.7 14.6 %collective-permute-start.5 = (bf16[4,36864]{1,0:T(4,128)(2,1)}, bf16[4,36864]{1,0:T(4,128)(2,1)}, u32[]{:S(2)}, u32[]{:S(2)}) collective-permute-start(bf16[4,36864]{1,0:T(4,128)(2,1)} %collective-permute-done.4), channel_id=1, source_target_pairs={{0,8},{8,0},{1,9},{9,1},{2,10},{10,2},{3,11},{11,3},{4,12},{12,4},... | collective-permute-start | bytes 884744 | tf_op jit(solution)/shard_map/ppermute | solution.py:144
  114.2 11.8 %collective-permute-start.8 = (bf16[4,36864]{1,0:T(4,128)(2,1)}, bf16[4,36864]{1,0:T(4,128)(2,1)}, u32[]{:S(2)}, u32[]{:S(2)}) collective-permute-start(bf16[4,36864]{1,0:T(4,128)(2,1)} %collective-permute-done.6), channel_id=1, source_target_pairs={{0,32},{8,488},{16,48},{24,504},{32,64},{40,8},{48,80},{56,24},{64... | collective-permute-start | bytes 884744 | tf_op jit(solution)/shard_map/ppermute | solution.py:141
  116.2 14.5 %collective-permute-start.7 = (bf16[4,36864]{1,0:T(4,128)(2,1)}, bf16[4,36864]{1,0:T(4,128)(2,1)}, u32[]{:S(2)}, u32[]{:S(2)}) collective-permute-start(bf16[4,36864]{1,0:T(4,128)(2,1)} %collective-permute-done.6), channel_id=1, source_target_pairs={{0,8},{8,0},{1,9},{9,1},{2,10},{10,2},{3,11},{11,3},{4,12},{12,4},... | collective-permute-start | bytes 884744 | tf_op jit(solution)/shard_map/ppermute | solution.py:144
  141.6 13.7 %collective-permute-start.10 = (bf16[4,36864]{1,0:T(4,128)(2,1)}, bf16[4,36864]{1,0:T(4,128)(2,1)}, u32[]{:S(2)}, u32[]{:S(2)}) collective-permute-start(bf16[4,36864]{1,0:T(4,128)(2,1)} %collective-permute-done.8), channel_id=1, source_target_pairs={{0,32},{8,488},{16,48},{24,504},{32,64},{40,8},{48,80},{56,24},{64... | collective-permute-start | bytes 884744 | tf_op jit(solution)/shard_map/ppermute | solution.py:141
  144.0 16.1 %collective-permute-start.9 = (bf16[4,36864]{1,0:T(4,128)(2,1)}, bf16[4,36864]{1,0:T(4,128)(2,1)}, u32[]{:S(2)}, u32[]{:S(2)}) collective-permute-start(bf16[4,36864]{1,0:T(4,128)(2,1)} %collective-permute-done.8), channel_id=1, source_target_pairs={{0,8},{8,0},{1,9},{9,1},{2,10},{10,2},{3,11},{11,3},{4,12},{12,4},... | collective-permute-start | bytes 884744 | tf_op jit(solution)/shard_map/ppermute | solution.py:144
  171.0 11.3 %collective-permute-start.12 = (bf16[4,36864]{1,0:T(4,128)(2,1)}, bf16[4,36864]{1,0:T(4,128)(2,1)}, u32[]{:S(2)}, u32[]{:S(2)}) collective-permute-start(bf16[4,36864]{1,0:T(4,128)(2,1)} %collective-permute-done.10), channel_id=1, source_target_pairs={{0,32},{8,488},{16,48},{24,504},{32,64},{40,8},{48,80},{56,24},{64... | collective-permute-start | bytes 884744 | tf_op jit(solution)/shard_map/ppermute | solution.py:141
  172.9 14.0 %collective-permute-start.11 = (bf16[4,36864]{1,0:T(4,128)(2,1)}, bf16[4,36864]{1,0:T(4,128)(2,1)}, u32[]{:S(2)}, u32[]{:S(2)}) collective-permute-start(bf16[4,36864]{1,0:T(4,128)(2,1)} %collective-permute-done.10), channel_id=1, source_target_pairs={{0,8},{8,0},{1,9},{9,1},{2,10},{10,2},{3,11},{11,3},{4,12},{12,4},... | collective-permute-start | bytes 884744 | tf_op jit(solution)/shard_map/ppermute | solution.py:144
  197.9 12.5 %collective-permute-start.14 = (bf16[4,36864]{1,0:T(4,128)(2,1)}, bf16[4,36864]{1,0:T(4,128)(2,1)}, u32[]{:S(2)}, u32[]{:S(2)}) collective-permute-start(bf16[4,36864]{1,0:T(4,128)(2,1)} %collective-permute-done.12), channel_id=1, source_target_pairs={{0,32},{8,488},{16,48},{24,504},{32,64},{40,8},{48,80},{56,24},{64... | collective-permute-start | bytes 884744 | tf_op jit(solution)/shard_map/ppermute | solution.py:141
  200.5 15.2 %collective-permute-start.13 = (bf16[4,36864]{1,0:T(4,128)(2,1)}, bf16[4,36864]{1,0:T(4,128)(2,1)}, u32[]{:S(2)}, u32[]{:S(2)}) collective-permute-start(bf16[4,36864]{1,0:T(4,128)(2,1)} %collective-permute-done.12), channel_id=1, source_target_pairs={{0,8},{8,0},{1,9},{9,1},{2,10},{10,2},{3,11},{11,3},{4,12},{12,4},... | collective-permute-start | bytes 884744 | tf_op jit(solution)/shard_map/ppermute | solution.py:144
  221.4 2.7 copy-start.2
  221.4 2.7 copy-start.5
  234.9 18.8 %copy-start = (bf16[2,256,384]{2,1,0:T(8,128)(2,1)S(1)}, bf16[2,256,384]{2,1,0:T(8,128)(2,1)}, u32[]{:S(2)}) copy-start(bf16[2,256,384]{2,1,0:T(8,128)(2,1)} %convolution_convert_fusion.2) | copy-start | bytes 1179652
  234.9 18.9 %copy-start.1 = (f32[2,256,384]{2,1,0:T(8,128)S(1)}, f32[2,256,384]{2,1,0:T(8,128)}, u32[]{:S(2)}) copy-start(f32[2,256,384]{2,1,0:T(8,128)} %fusion.64) | copy-start | bytes 2359300
  236.9 10.3 %collective-permute-start.15 = (bf16[2,128,384]{2,1,0:T(8,128)(2,1)S(1)}, bf16[2,128,384]{2,1,0:T(8,128)(2,1)S(1)}, u32[]{:S(2)}, u32[]{:S(2)}) collective-permute-start(bf16[2,128,384]{2,1,0:T(8,128)(2,1)S(1)} %slice.249), channel_id=1, source_target_pairs={{0,8},{8,16},{16,24},{24,32},{32,40},{40,48},{48,56},{56,64},{64,7... | collective-permute-start | bytes 589832 | tf_op jit(solution)/shard_map/ppermute | solution.py:40
  243.1 10.6 %collective-permute-start.16 = (bf16[2,128,384]{2,1,0:T(8,128)(2,1)S(1)}, bf16[2,128,384]{2,1,0:T(8,128)(2,1)S(1)}, u32[]{:S(2)}, u32[]{:S(2)}) collective-permute-start(bf16[2,128,384]{2,1,0:T(8,128)(2,1)S(1)} %slice.252), channel_id=1, source_target_pairs={{8,0},{16,8},{24,16},{32,24},{40,32},{48,40},{56,48},{64,56},{72,6... | collective-permute-start | bytes 589832 | tf_op jit(solution)/shard_map/ppermute | solution.py:41
  248.2 5.7 %copy-start.3 = (bf16[1,256,768]{2,1,0:T(8,128)(2,1)S(1)}, bf16[1,256,768]{2,1,0:T(8,128)(2,1)}, u32[]{:S(2)}) copy-start(bf16[1,256,768]{2,1,0:T(8,128)(2,1)} %param.5) | copy-start | bytes 1179652
  248.2 5.7 %copy-start.6 = (bf16[1,256,768]{2,1,0:T(8,128)(2,1)S(1)}, bf16[1,256,768]{2,1,0:T(8,128)(2,1)}, u32[]{:S(2)}) copy-start(bf16[1,256,768]{2,1,0:T(8,128)(2,1)} %param.6) | copy-start | bytes 1179652
  256.4 10.6 %collective-permute-start.17 = (bf16[2,256,384]{2,1,0:T(8,128)(2,1)S(1)}, bf16[2,256,384]{2,1,0:T(8,128)(2,1)S(1)}, u32[]{:S(2)}, u32[]{:S(2)}) collective-permute-start(bf16[2,256,384]{2,1,0:T(8,128)(2,1)S(1)} %convolution_convert_fusion.1), channel_id=1, source_target_pairs={{0,16},{8,24},{16,32},{24,40},{32,48},{40,56},{48,64},{56,72},{64,... | collective-permute-start | bytes 1179656 | tf_op jit(solution)/shard_map/ppermute | solution.py:49
  259.0 15.9 %collective-permute-start.18 = (bf16[2,256,384]{2,1,0:T(8,128)(2,1)S(1)}, bf16[2,256,384]{2,1,0:T(8,128)(2,1)S(1)}, u32[]{:S(2)}, u32[]{:S(2)}) collective-permute-start(bf16[2,256,384]{2,1,0:T(8,128)(2,1)S(1)} %convolution_convert_fusion), channel_id=1, source_target_pairs={{16,0},{24,8},{32,16},{40,24},{48,32},{56,40},{64,48},{72,56},{80,... | collective-permute-start | bytes 1179656 | tf_op jit(solution)/shard_map/ppermute | solution.py:49
  264.6 10.4 %copy-start.4 = (bf16[1,256,768]{2,1,0:T(8,128)(2,1)S(1)}, bf16[1,256,768]{2,1,0:T(8,128)(2,1)}, u32[]{:S(2)}) copy-start(bf16[1,256,768]{2,1,0:T(8,128)(2,1)} %param.7) | copy-start | bytes 1179652
  276.6 14.6 %collective-permute-start.21 = (bf16[1,256,384]{2,1,0:T(8,128)(2,1)S(1)}, bf16[1,256,384]{2,1,0:T(8,128)(2,1)S(1)}, u32[]{:S(2)}, u32[]{:S(2)}) collective-permute-start(bf16[1,256,384]{2,1,0:T(8,128)(2,1)S(1)} %fusion.101), channel_id=1, source_target_pairs={{0,16},{8,24},{16,32},{24,40},{32,48},{40,56},{48,64},{56,72},{64,... | collective-permute-start | bytes 589832 | tf_op jit(solution)/shard_map/ppermute | solution.py:49
  285.0 11.3 %collective-permute-start.20 = (bf16[1,256,384]{2,1,0:T(8,128)(2,1)S(1)}, bf16[1,256,384]{2,1,0:T(8,128)(2,1)S(1)}, u32[]{:S(2)}, u32[]{:S(2)}) collective-permute-start(bf16[1,256,384]{2,1,0:T(8,128)(2,1)S(1)} %fusion.101), channel_id=1, source_target_pairs={{16,0},{24,8},{32,16},{40,24},{48,32},{56,40},{64,48},{72,56},{80,... | collective-permute-start | bytes 589832 | tf_op jit(solution)/shard_map/ppermute | solution.py:49
  288.7 28.6 %collective-permute-start.19 = (bf16[1,256,768]{2,1,0:T(8,128)(2,1)S(1)}, bf16[1,256,768]{2,1,0:T(8,128)(2,1)S(1)}, u32[]{:S(2)}, u32[]{:S(2)}) collective-permute-start(bf16[1,256,768]{2,1,0:T(8,128)(2,1)S(1)} %fusion.55), channel_id=1, source_target_pairs={{7,0},{0,1},{1,2},{2,3},{3,4},{4,5},{5,6},{6,7},{15,8},{8,9},{9,10... | collective-permute-start | bytes 1179656 | tf_op jit(solution)/shard_map/ppermute | solution.py:55
  298.7 8.0 %collective-permute-start.23 = (bf16[1,128,384]{2,1,0:T(8,128)(2,1)S(1)}, bf16[1,128,384]{2,1,0:T(8,128)(2,1)S(1)}, u32[]{:S(2)}, u32[]{:S(2)}) collective-permute-start(bf16[1,128,384]{2,1,0:T(8,128)(2,1)S(1)} %get-tuple-element.3), channel_id=1, source_target_pairs={{0,8},{8,16},{16,24},{24,32},{32,40},{40,48},{48,56},{56,64},{64,7... | collective-permute-start | bytes 294920 | tf_op jit(solution)/shard_map/ppermute | solution.py:40
  304.8 9.6 %collective-permute-start.22 = (bf16[1,128,384]{2,1,0:T(8,128)(2,1)S(1)}, bf16[1,128,384]{2,1,0:T(8,128)(2,1)S(1)}, u32[]{:S(2)}, u32[]{:S(2)}) collective-permute-start(bf16[1,128,384]{2,1,0:T(8,128)(2,1)S(1)} %get-tuple-element.2), channel_id=1, source_target_pairs={{8,0},{16,8},{24,16},{32,24},{40,32},{48,40},{56,48},{64,56},{72,6... | collective-permute-start | bytes 294920 | tf_op jit(solution)/shard_map/ppermute | solution.py:41
  315.2 10.9 %collective-permute-start.24 = (bf16[1,256,768]{2,1,0:T(8,128)(2,1)S(1)}, bf16[1,256,768]{2,1,0:T(8,128)(2,1)S(1)}, u32[]{:S(2)}, u32[]{:S(2)}) collective-permute-start(bf16[1,256,768]{2,1,0:T(8,128)(2,1)S(1)} %fusion.24), channel_id=1, source_target_pairs={{1,0},{2,1},{3,2},{4,3},{5,4},{6,5},{7,6},{0,7},{9,8},{10,9},{11,1... | collective-permute-start | bytes 1179656 | tf_op jit(solution)/shard_map/ppermute | solution.py:55
